TPU v7x, 32 devices: a whole 2x2x4 slice. The times are simulated.
32 devices in a mesh: ctx: 8 (over y, x, core), tp: 4 (over z).
Axes of the slice: x: 2, y: 2, z: 4, core: 2. Of those that a mesh axis runs over, the one named last changes fastest.
Arguments:
- stream: bfloat16 [1024, 4096], P('ctx', 'tp'), may hold values from -52 to 52
- shutter: bfloat16 [1024, 4096], P('ctx', 'tp'), may hold values from -6 to 6
- feeder: bfloat16 [1024, 4096], P('ctx', 'tp'), may hold values from -6 to 6
- stencil: float32 [7, 4096], P(None, 'tp'), may hold values from -2 to 2
- valves: bfloat16 [1024, 4096], P('ctx', 'tp'), may hold values from -6 to 6
- intake: bfloat16 [1024, 4096], P('ctx', 'tp'), may hold values from -6 to 6
- kernel: float32 [128, 4096], P(None, 'tp'), may hold values from -0.5 to 0.5
- scaling: float32 [4096], P('tp'), may hold values from 0.1 to 1.9
- queries: bfloat16 [1024, 4096], P('ctx', 'tp'), may hold values from -87 to 87
- matchers: bfloat16 [1024, 4096], P('ctx', 'tp'), may hold values from -6 to 6
- segments: int32 [1024], replicated, may hold values from 0 to 3, never falling along the last dimension, each value on 1 to 768 neighbouring positions
- cotangent: bfloat16 [1024, 4096], P('ctx', 'tp'), may hold values from -6 to 6
Outputs:
- result: bfloat16 [1024, 4096], P('ctx', 'tp')
- stream_grad: bfloat16 [1024, 4096], P('ctx', 'tp')
- shutter_grad: bfloat16 [1024, 4096], P('ctx', 'tp')
- feeder_grad: bfloat16 [1024, 4096], P('ctx', 'tp')
- stencil_grad: float32 [7, 4096], P(None, 'tp')
- valves_grad: bfloat16 [1024, 4096], P('ctx', 'tp')
- intake_grad: bfloat16 [1024, 4096], P('ctx', 'tp')
- kernel_grad: float32 [128, 4096], P(None, 'tp')
- scaling_grad: float32 [4096], P('tp')
- queries_grad: bfloat16 [1024, 4096], P('ctx', 'tp')
- matchers_grad: bfloat16 [1024, 4096], P('ctx', 'tp')
Inputs may be any that keep to these rules, and one draw needn't show every extreme that they name: `segments`: document numbers never fall along the context; each of the 4 documents covers 1 to 768 positions, and one covers exactly 768.
All inputs are finite; a program needn't handle non-finite values.
Results may differ from a plain program's by a relative error of at most 0.03.
Values may be sent and summed in bfloat16 or wider, within the bound.
No kernel may reach another device: no remote copies, remote signals or barrier semaphores. Data moves between devices by JAX's collectives and lax.ppermute only.
A program may use at most 192 MiB of HBM per device.

v0:
```python
import math
import jax
import jax.numpy as jnp
from jax import lax
from jax.sharding import PartitionSpec as P

HD = 128
D = 4096
KS = 7
KM = 128
epsilon = 1e-06


def as_sent(shard):

    def short(part):
        return part.astype(jnp.bfloat16) if part.dtype == jnp.float32 else part

    return jax.tree.map(short, shard)


def passed_along(value, axis, steps):
    count = lax.axis_size(axis)
    leading, last = (max(0, -steps), min(count, count - steps))
    return lax.ppermute(value, axis, [(source, source + steps) for source in range(leading, last)])


def depthwise(padded, tap_rows):
    return lax.conv_general_dilated(
        padded[None],
        tap_rows[:, None, :],
        (1,),
        "VALID",
        dimension_numbers=("NWC", "WIO", "NWC"),
        feature_group_count=padded.shape[1],
        precision=lax.Precision.HIGHEST,
    )[0]


def neighbor_rows(edge_rows, offset):
    return passed_along(as_sent(edge_rows), "ctx", offset).astype(edge_rows.dtype)


def channel_total(partial_value):
    return lax.psum(partial_value, "tp")


def shards(
    stream,
    shutter,
    feeder,
    stencil,
    valves,
    intake,
    kernel,
    scaling,
    queries,
    matchers,
    segments,
    cotangent,
):
    local_rows = stream.shape[0]
    width_local = stream.shape[1]
    head_count = width_local // HD
    total_rows = local_rows * lax.axis_size("ctx")
    position = lax.axis_index("ctx") * local_rows
    scale_factor = 1.0 / math.sqrt(HD)
    widened = stream.astype(jnp.float32)
    inner_one = feeder.astype(jnp.float32) * widened
    rim_one = neighbor_rows(inner_one[local_rows - (KS - 1) :], 1)
    padded_one = jnp.concatenate([rim_one, inner_one], axis=0)
    conv_one = depthwise(padded_one, stencil[::-1])
    first_out = (widened + shutter.astype(jnp.float32) * conv_one).astype(jnp.bfloat16)
    first_wide = first_out.astype(jnp.float32)
    inner_two = intake.astype(jnp.float32) * first_wide
    rim_two = neighbor_rows(inner_two[local_rows - (KM - 1) :], 1)
    padded_two = jnp.concatenate([rim_two, inner_two], axis=0)
    conv_two = depthwise(padded_two, kernel[::-1])
    second_out = (first_wide + valves.astype(jnp.float32) * conv_two).astype(jnp.bfloat16)
    second_wide = second_out.astype(jnp.float32)
    squares = channel_total(jnp.sum(second_wide * second_wide, axis=1))
    inverse_rms = lax.rsqrt(squares / D + epsilon)
    normed = (second_wide * inverse_rms[:, None] * scaling).astype(jnp.bfloat16)
    keys_whole, values_whole = (
        lax.all_gather(matchers, "ctx", axis=0, tiled=True),
        lax.all_gather(normed, "ctx", axis=0, tiled=True),
    )
    query_pos = position + jnp.arange(local_rows, dtype=jnp.int32)
    key_pos = jnp.arange(total_rows, dtype=jnp.int32)
    query_seg = lax.dynamic_slice_in_dim(segments, position, local_rows, 0)
    visible = (key_pos[None, :] <= query_pos[:, None]) & (segments[None, :] == query_seg[:, None])
    contract = (((1,), (1,)), ((), ()))
    weight_list = []
    dscore_list = []
    attended_list = []
    query_grad_list = []
    logsum_list = []
    delta_list = []
    for head_index in range(head_count):
        columns = slice(head_index * HD, (head_index + 1) * HD)
        query_head = queries[:, columns]
        key_head = keys_whole[:, columns]
        value_head = values_whole[:, columns]
        cotangent_head = cotangent[:, columns]
        scores = (
            lax.dot_general(query_head, key_head, contract, preferred_element_type=jnp.float32)
            * scale_factor
        )
        scores = jnp.where(visible, scores, -jnp.inf)
        row_max = jnp.max(scores, axis=1)
        logsum = row_max + jnp.log(jnp.sum(jnp.exp(scores - row_max[:, None]), axis=1))
        weights = jnp.exp(scores - logsum[:, None]).astype(jnp.bfloat16)
        attended = jnp.dot(weights, value_head, preferred_element_type=jnp.float32)
        weight_grad = lax.dot_general(
            cotangent_head, value_head, contract, preferred_element_type=jnp.float32
        )
        row_delta = jnp.sum(cotangent_head.astype(jnp.float32) * attended, axis=1)
        dscore = (
            scale_factor * weights.astype(jnp.float32) * (weight_grad - row_delta[:, None])
        ).astype(jnp.bfloat16)
        query_grad = jnp.dot(dscore, key_head, preferred_element_type=jnp.float32)
        weight_list.append(weights)
        dscore_list.append(dscore)
        attended_list.append(attended)
        query_grad_list.append(query_grad)
        logsum_list.append(logsum)
        delta_list.append(row_delta)
    attended_all = jnp.concatenate(attended_list, axis=1)
    result = (second_wide + attended_all).astype(jnp.bfloat16)
    queries_grad = jnp.concatenate(query_grad_list, axis=1).astype(jnp.bfloat16)
    query_heads = queries.reshape(local_rows, head_count, HD)
    cotangent_heads = cotangent.reshape(local_rows, head_count, HD)
    weights_all = jnp.stack(weight_list)
    dscore_all = jnp.stack(dscore_list)
    dscore_part = lax.slice_in_dim(dscore_all, 0, local_rows * lax.axis_size("ctx"), axis=2)
    key_part = jnp.einsum(
        "hts,the->she", dscore_part, query_heads, preferred_element_type=jnp.float32
    )
    value_part = jnp.einsum(
        "hts,the->she", weights_all, cotangent_heads, preferred_element_type=jnp.float32
    )
    summed = lax.psum_scatter(
        jnp.concatenate(
            [
                key_part.reshape(local_rows * lax.axis_size("ctx"), width_local),
                value_part.reshape(local_rows * lax.axis_size("ctx"), width_local),
            ],
            axis=1,
        ).astype(jnp.bfloat16),
        "ctx",
        scatter_dimension=0,
        tiled=True,
    ).astype(jnp.float32)
    matchers_grad = summed[:, :width_local].astype(jnp.bfloat16)
    value_grad = summed[:, width_local:]
    gain_part = value_grad * scaling
    projected = channel_total(jnp.sum(gain_part * second_wide, axis=1))
    scaling_part = jnp.sum(value_grad * second_wide * inverse_rms[:, None], axis=0)
    second_grad = (
        cotangent.astype(jnp.float32)
        + inverse_rms[:, None] * gain_part
        - second_wide * (inverse_rms**3 * projected / D)[:, None]
    )
    valves_grad = (second_grad * conv_two).astype(jnp.bfloat16)
    dconv_two = second_grad * valves.astype(jnp.float32)
    back_two = neighbor_rows(dconv_two[: KM - 1], -1)
    dinner_two = depthwise(jnp.concatenate([dconv_two, back_two], axis=0), kernel)
    intake_grad = (dinner_two * first_wide).astype(jnp.bfloat16)
    kernel_part = depthwise(padded_two, dconv_two)[::-1]
    first_grad = second_grad + dinner_two * intake.astype(jnp.float32)
    shutter_grad = (first_grad * conv_one).astype(jnp.bfloat16)
    dconv_one = first_grad * shutter.astype(jnp.float32)
    back_one = neighbor_rows(dconv_one[: KS - 1], -1)
    dinner_one = depthwise(jnp.concatenate([dconv_one, back_one], axis=0), stencil)
    feeder_grad = (dinner_one * widened).astype(jnp.bfloat16)
    stencil_part = depthwise(padded_one, dconv_one)[::-1]
    stream_grad = (first_grad + dinner_one * feeder.astype(jnp.float32)).astype(jnp.bfloat16)
    stencil_sum, kernel_sum, scaling_sum = (
        lax.psum(stencil_part.astype(jnp.bfloat16), "ctx").astype(jnp.float32),
        lax.psum(kernel_part.astype(jnp.bfloat16), "ctx").astype(jnp.float32),
        lax.psum(scaling_part.astype(jnp.bfloat16), "ctx").astype(jnp.float32),
    )
    normalizer = math.sqrt(total_rows)
    return (
        result,
        stream_grad,
        shutter_grad,
        feeder_grad,
        stencil_sum / normalizer,
        valves_grad,
        intake_grad,
        kernel_sum / normalizer,
        scaling_sum / normalizer,
        queries_grad,
        matchers_grad,
    )


def solution(mesh):
    placed = (
        P("ctx", "tp"),
        P("ctx", "tp"),
        P("ctx", "tp"),
        P(None, "tp"),
        P("ctx", "tp"),
        P("ctx", "tp"),
        P(None, "tp"),
        P("tp"),
        P("ctx", "tp"),
        P("ctx", "tp"),
        P(),
        P("ctx", "tp"),
    )
    return jax.shard_map(
        shards,
        mesh=mesh,
        in_specs=placed,
        out_specs=(
            P("ctx", "tp"),
            P("ctx", "tp"),
            P("ctx", "tp"),
            P("ctx", "tp"),
            P(None, "tp"),
            P("ctx", "tp"),
            P("ctx", "tp"),
            P(None, "tp"),
            P("tp"),
            P("ctx", "tp"),
            P("ctx", "tp"),
        ),
        check_vma=False,
    )
```

profile of v0, /device:TPU:0, one launch (start us, length us, event | category | flops | bytes accessed | tf_op | source)
XLA Modules:
  0.0 272.9 jit_solution(10646670163490515569)
XLA Ops:
  9.1 2.4 collective-permute-start
  11.4 2.8 %rev.12 = f32[7,1024]{1,0:T(8,128)S(1)} reverse(f32[7,1024]{1,0:T(8,128)} %param.15), dimensions={0} | reverse | bytes 57344 | tf_op jit(solution)/shard_map/rev | solution.py:72
  18.3 4.5 %collective-permute-start.1 = (bf16[127,1024]{1,0:T(8,128)(2,1)}, bf16[127,1024]{1,0:T(8,128)(2,1)S(1)}, u32[]{:S(2)}, u32[]{:S(2)}) collective-permute-start(bf16[127,1024]{1,0:T(8,128)(2,1)} %slice.349), channel_id=1, source_target_pairs={{0,4},{4,8},{8,12},{12,16},{16,20},{20,24},{24,28},{1,5},{5,9},{9,... | collective-permute-start | bytes 780296 | tf_op jit(solution)/shard_map/ppermute | solution.py:25
  25.1 5.6 %fusion.74 = f32[1,128,1024]{2,0,1:T(1,128)S(1)} fusion(f32[1,255,1024]{2,0,1:T(1,128)S(1)} %broadcast_in_dim.33, f32[128,1,1024]{2,0,1:T(8,128)S(1)} %bitcast.165), kind=kOutput, calls=%fused_computation.133 | convolution fusion | flops 201326592 | bytes 2093056 | tf_op jit(solution)/shard_map/conv_general_dilated | solution.py:29
  31.6 11.9 %psum.35 = f32[128]{0:T(128)S(1)} all-reduce(f32[128]{0:T(128)S(1)} %get-tuple-element.63), channel_id=1, replica_groups=mesh['ctx'=8,'tp'=4] {'tp'}, use_global_device_ids=true, to_apply=%region_3.4 | all-reduce | flops 128 | bytes 1024 | tf_op jit(solution)/shard_map/psum | solution.py:45
  64.7 2.6 copy.116
  67.3 7.6 %all-gather.5.cloned.1.call-done = bf16[1024,1024]{1,0:T(8,128)(2,1)} async-done(((bf16[128,1024]{1,0:T(8,128)(2,1)}), bf16[1024,1024]{1,0:T(8,128)(2,1)}) %all-gather.5.cloned.1.call-update) | async-done | bytes 2097168 | tf_op jit(solution)/shard_map/all_gather | solution.py:86
  91.7 2.6 copy.114
  94.3 4.7 %pad_maximum_fusion = bf16[1024,2048]{1,0:T(8,128)(2,1)} fusion(bf16[1024,1024]{1,0:T(8,128)(2,1)} %copy.116, bf16[1024,1024]{1,0:T(8,128)(2,1)} %copy.114), kind=kLoop, calls=%fused_computation | loop fusion | flops 8388608 | bytes 8388608 | tf_op jit(solution)/shard_map/concatenate | solution.py:143
  111.6 1.9 fusion.39
  113.5 1.9 fusion.38
  115.4 1.8 fusion.37
  117.2 1.8 fusion.36
  119.1 1.9 fusion.35
  120.9 1.9 fusion.34
  124.7 25.8 %reduce-scatter.2.cloned.1.call-done = bf16[128,2048]{1,0:T(8,128)(2,1)} async-done(((bf16[1024,2048]{1,0:T(8,128)(2,1)}), bf16[128,2048]{1,0:T(8,128)(2,1)}) %reduce-scatter.2.cloned.1.call-update) | async-done | bytes 524304 | tf_op jit(solution)/shard_map/reduce_scatter | solution.py:142
  151.7 11.7 %psum.36 = f32[128]{0:T(128)S(1)} all-reduce(f32[128]{0:T(128)S(1)} %get-tuple-element.34), channel_id=1, replica_groups=mesh['ctx'=8,'tp'=4] {'tp'}, use_global_device_ids=true, to_apply=%region_28.29 | all-reduce | flops 128 | bytes 1024 | tf_op jit(solution)/shard_map/psum | solution.py:45
  164.6 6.8 %fusion.70 = bf16[1,128,1024]{2,0,1:T(2,128)(2,1)S(1)} fusion(f32[1,255,1024]{2,0,1:T(1,128)} %copy-done.30, f32[128,1,1024]{2,0,1:T(8,128)S(1)} %bitcast.159), kind=kOutput, calls=%fused_computation.129 | convolution fusion | flops 201326592 | bytes 1830912 | tf_op jit(solution)/shard_map/conv_general_dilated | solution.py:29
  171.5 2.6 rev.15
  179.4 45.7 %all-reduce.3.cloned.1.call-done = bf16[128,1024]{1,0:T(8,128)(2,1)} async-done(((bf16[128,1024]{1,0:T(8,128)(2,1)}), bf16[128,1024]{1,0:T(8,128)(2,1)}) %all-reduce.3.cloned.1.call-update) | async-done | bytes 262160 | tf_op jit(solution)/shard_map/psum | solution.py:180
  225.1 1.8 convert_multiply_fusion.16
  227.1 5.8 %fusion.40 = f32[1,128,1024]{2,0,1:T(1,128)S(1)} fusion(f32[1,255,1024]{2,1,0:T(8,128)S(1)} %maximum_bitcast_fusion, f32[128,1,1024]{2,0,1:T(8,128)S(1)} %bitcast.164), kind=kOutput, calls=%fused_computation.77 | convolution fusion | flops 201326592 | bytes 2093056 | tf_op jit(solution)/shard_map/conv_general_dilated | solution.py:29
  232.9 2.7 %multiply_convert_fusion = (bf16[128,1024]{1,0:T(8,128)(2,1)}, f32[128,1024]{1,0:T(8,128)S(1)}, bf16[128,1024]{1,0:T(8,128)(2,1)}, bf16[128,1024]{1,0:T(8,128)(2,1)}, bf16[128,1024]{1,0:T(8,128)(2,1)}) fusion(f32[1,136,1024]{2,1,0:T(8,128)S(1)} %reshape.119, bf16[128,1024]{1,0:T(8,128)(2,1)S(1)} %copy-done.26, f32[1,128,1024]{2,0,1:T(1,128)S(1)} %fusion.40, ...), kind=kLoop, calls=%fused_computation.136 | loop fusion | flops 2621440 | bytes 4985856 | tf_op jit(solution)/shard_map/convert_element_type | solution.py:171
  237.1 22.4 %all-reduce = (bf16[7,1024]{1,0:T(8,128)(2,1)S(1)}, bf16[1024]{0:T(1024)(128)(2,1)S(1)}) all-reduce(bf16[7,1024]{1,0:T(8,128)(2,1)S(1)} %rev.14, bf16[1024]{0:T(1024)(128)(2,1)S(1)} %get-tuple-element.33), channel_id=1, replica_groups=mesh['ctx'=8,'tp'=4] {'ctx'}, use_global_device_ids=true, to_apply=%region_29.30 | all-reduce | flops 8192 | bytes 32768 | tf_op jit(solution)/shard_map/psum | solution.py:179
  (215 shorter events, 77.0 us)
Async XLA Ops:
  7.2 37.5 %all-gather.3.cloned.1.call-start = ((), (), s32[]{:S(2)}) async-start(), calls=%async_computation.1 | async-start | bytes 2359296 | tf_op jit(solution)/shard_map/all_gather | solution.py:85
  7.9 67.0 %all-gather.5.cloned.1.call-start = ((), (), s32[]{:S(2)}) async-start(), calls=%async_computation.2 | async-start | bytes 2359296 | tf_op jit(solution)/shard_map/all_gather | solution.py:86
  9.1 5.2 %collective-permute-start = (bf16[6,1024]{1,0:T(8,128)(2,1)S(1)}, bf16[6,1024]{1,0:T(8,128)(2,1)S(1)}, u32[]{:S(2)}, u32[]{:S(2)}) collective-permute-start(bf16[6,1024]{1,0:T(8,128)(2,1)S(1)} %slice.351), channel_id=1, source_target_pairs={{0,4},{4,8},{8,12},{12,16},{16,20},{20,24},{24,28},{1,5},{5,9},{9,... | collective-permute-start | bytes 36872 | tf_op jit(solution)/shard_map/ppermute | solution.py:25
  16.6 6.2 %copy-start.33 = (f32[128,1024]{1,0:T(8,128)S(1)}, f32[128,1024]{1,0:T(8,128)}, u32[]{:S(2)}) copy-start(f32[128,1024]{1,0:T(8,128)} %param.18) | copy-start | bytes 1572868
  17.4 5.9 %copy-start.36 = (bf16[128,1024]{1,0:T(8,128)(2,1)S(1)}, bf16[128,1024]{1,0:T(8,128)(2,1)}, u32[]{:S(2)}) copy-start(bf16[128,1024]{1,0:T(8,128)(2,1)} %param.20) | copy-start | bytes 786436
  17.4 6.8 %copy-start.39 = (s32[1024]{0:T(1024)S(1)}, s32[1024]{0:T(1024)}, u32[]{:S(2)}) copy-start(s32[1024]{0:T(1024)} %param.22) | copy-start | bytes 12292
  17.5 13.3 %copy-start.2 = (bf16[128,1024]{1,0:T(8,128)(2,1)}, bf16[128,1024]{1,0:T(8,128)(2,1)S(1)}, u32[]{:S(2)}) copy-start(bf16[128,1024]{1,0:T(8,128)(2,1)S(1)} %get-tuple-element.66) | copy-start | bytes 786436
  18.3 5.9 %collective-permute-start.1 = (bf16[127,1024]{1,0:T(8,128)(2,1)}, bf16[127,1024]{1,0:T(8,128)(2,1)S(1)}, u32[]{:S(2)}, u32[]{:S(2)}) collective-permute-start(bf16[127,1024]{1,0:T(8,128)(2,1)} %slice.349), channel_id=1, source_target_pairs={{0,4},{4,8},{8,12},{12,16},{16,20},{20,24},{24,28},{1,5},{5,9},{9,... | collective-permute-start | bytes 780296 | tf_op jit(solution)/shard_map/ppermute | solution.py:25
  25.1 18.4 %copy-start.37 = (f32[1024]{0:T(1024)S(1)}, f32[1024]{0:T(1024)}, u32[]{:S(2)}) copy-start(f32[1024]{0:T(1024)} %param.19) | copy-start | bytes 12292
  44.4 106.1 %reduce-scatter.2.cloned.1.call-start = ((), (), s32[]{:S(2)}) async-start(), calls=%async_computation.3 | async-start | bytes 4718592 | tf_op jit(solution)/shard_map/reduce_scatter | solution.py:142
  67.3 14.2 %copy-start.4 = (bf16[128,1024]{1,0:T(8,128)(2,1)S(1)}, bf16[128,1024]{1,0:T(8,128)(2,1)}, u32[]{:S(2)}) copy-start(bf16[128,1024]{1,0:T(8,128)(2,1)} %get-tuple-element.60) | copy-start | bytes 786436
  74.9 6.9 %copy-start.24 = (bf16[128,1024]{1,0:T(8,128)(2,1)S(1)}, bf16[128,1024]{1,0:T(8,128)(2,1)}, u32[]{:S(2)}) copy-start(bf16[128,1024]{1,0:T(8,128)(2,1)} %get-tuple-element.62) | copy-start | bytes 786436
  74.9 7.3 %copy-start.10 = (bf16[128,1024]{1,0:T(8,128)(2,1)S(1)}, bf16[128,1024]{1,0:T(8,128)(2,1)}, u32[]{:S(2)}) copy-start(bf16[128,1024]{1,0:T(8,128)(2,1)} %get-tuple-element.48) | copy-start | bytes 786436
  99.0 12.6 %copy-start.17 = (bf16[1024,1024]{1,0:T(8,128)(2,1)S(1)}, bf16[1024,1024]{1,0:T(8,128)(2,1)}, u32[]{:S(2)}) copy-start(bf16[1024,1024]{1,0:T(8,128)(2,1)} %all-gather.3.cloned.1.call-done) | copy-start | bytes 6291460
  99.0 126.1 %all-reduce.3.cloned.1.call-start = ((), (), s32[]{:S(2)}) async-start(), calls=%async_computation.4 | async-start | bytes 524288 | tf_op jit(solution)/shard_map/psum | solution.py:180
  104.3 18.6 %copy-start.22 = (bf16[128,1024]{1,0:T(8,128)(2,1)S(1)}, bf16[128,1024]{1,0:T(8,128)(2,1)}, u32[]{:S(2)}) copy-start(bf16[128,1024]{1,0:T(8,128)(2,1)} %get-tuple-element.102) | copy-start | bytes 786436
  110.3 13.4 %copy-start.23 = (bf16[128,1024]{1,0:T(8,128)(2,1)S(1)}, bf16[128,1024]{1,0:T(8,128)(2,1)}, u32[]{:S(2)}) copy-start(bf16[128,1024]{1,0:T(8,128)(2,1)} %get-tuple-element.104) | copy-start | bytes 786436
  113.5 49.9 %copy-start.21 = (bf16[128,1024]{1,0:T(8,128)(2,1)S(1)}, bf16[128,1024]{1,0:T(8,128)(2,1)}, u32[]{:S(2)}) copy-start(bf16[128,1024]{1,0:T(8,128)(2,1)} %param.16) | copy-start | bytes 786436
  164.6 10.2 %copy-start.35 = (f32[128,128]{0,1:T(8,128)S(1)}, f32[128,128]{0,1:T(8,128)}, u32[]{:S(2)}) copy-start(f32[128,128]{0,1:T(8,128)} %get-tuple-element.88) | copy-start | bytes 196612
  171.4 7.2 %copy-start.18 = (bf16[128,2048]{1,0:T(8,128)(2,1)S(1)}, bf16[128,2048]{1,0:T(8,128)(2,1)}, u32[]{:S(2)}) copy-start(bf16[128,2048]{1,0:T(8,128)(2,1)} %reduce-scatter.2.cloned.1.call-done) | copy-start | bytes 1572868
  174.9 51.9 %collective-permute-start.2 = (bf16[127,1024]{1,0:T(8,128)(2,1)S(1)}, bf16[127,1024]{1,0:T(8,128)(2,1)S(1)}, u32[]{:S(2)}, u32[]{:S(2)}) collective-permute-start(bf16[127,1024]{1,0:T(8,128)(2,1)S(1)} %slice.348), channel_id=1, source_target_pairs={{4,0},{8,4},{12,8},{16,12},{20,16},{24,20},{28,24},{5,1},{9,5},{13... | collective-permute-start | bytes 780296 | tf_op jit(solution)/shard_map/ppermute | solution.py:25
  178.7 48.4 %copy-start.34 = (f32[128,1024]{1,0:T(8,128)S(1)}, f32[128,1024]{1,0:T(8,128)}, u32[]{:S(2)}) copy-start(f32[128,1024]{1,0:T(8,128)} %param.18) | copy-start | bytes 1572868
  227.0 5.8 %copy-start.3 = (bf16[128,1024]{1,0:T(8,128)(2,1)S(1)}, bf16[128,1024]{1,0:T(8,128)(2,1)}, u32[]{:S(2)}) copy-start(bf16[128,1024]{1,0:T(8,128)(2,1)} %copy-done.2) | copy-start | bytes 786436
  260.1 3.1 %collective-permute-start.3 = (bf16[6,1024]{1,0:T(8,128)(2,1)S(1)}, bf16[6,1024]{1,0:T(8,128)(2,1)S(1)}, u32[]{:S(2)}, u32[]{:S(2)}) collective-permute-start(bf16[6,1024]{1,0:T(8,128)(2,1)S(1)} %slice.350), channel_id=1, source_target_pairs={{4,0},{8,4},{12,8},{16,12},{20,16},{24,20},{28,24},{5,1},{9,5},{13... | collective-permute-start | bytes 36872 | tf_op jit(solution)/shard_map/ppermute | solution.py:25
  (25 other events, 73.2 us)
Sparse Core Ops, SparseCore 0:
  9.9 30.5 all-gather.2
  44.5 30.3 all-gather.4
  99.1 51.3 reduce-scatter.1
  174.3 50.7 all-reduce.2
where the time goes:
time: 274 us; the launch traced here: 273 us
  waiting for transfers between devices  81 us (30%)
  matrix products  60.8 us (22%)
  blocking collectives  46 us (17%)
  local copies, waits for them, and re-layouts  35.2 us (13%)
  other arithmetic  25.2 us (9%)
  between operations  14.6 us (5%)
  starting transfers between devices  10 us (4%)
    psum x1, waiting for transfers between devices, shards(): lax.psum(kernel_part.astype(jnp.bfloat16), 'ctx').astype(jnp.float32)  45.7 us
    reduce_scatter x1, waiting for transfers between devices, shards(): lax.psum_scatter(jnp.concatenate([key_part.reshape(local_rows * lax.axis_...  25.8 us
    psum x2, blocking collectives, channel_total(): return lax.psum(partial_value, 'tp')  23.6 us
    psum x1, blocking collectives, shards(): lax.psum(stencil_part.astype(jnp.bfloat16), 'ctx').astype(jnp.float32)  22.4 us
    conv_general_dilated x6, matrix products, depthwise(): lax.conv_general_dilated(padded[None], tap_rows[:, None, :], (1,), 'VALID...  19.9 us
    dot_general x8, matrix products, shards(): query_grad = jnp.dot(dscore, key_head, preferred_element_type=jnp.float32)  13 us
    unnamed x93, local copies, waits for them, and re-layouts  12.7 us
    dot_general x8, matrix products, shards(): lax.dot_general(query_head, key_head, contract, preferred_element_type=jn...  10.6 us
  transfers between devices with their start and end apart: 8, of which 4 were waited for; matrix products, arithmetic and copies ran while one was open for 25% of the time, Pallas kernels for 0%

commit v1 on v0

--- a/solution.py
+++ b/solution.py
@@ -9,6 +9,19 @@
 KS = 7
 KM = 128
 epsilon = 1e-06
+
+
+def collect(array, axis, dim):
+    ways = lax.axis_size(axis)
+    up = [(d, (d + 1) % ways) for d in range(ways)]
+    down = [(d, (d - 1) % ways) for d in range(ways)]
+    earlier, later = ([array], [array])
+    for _ in range(ways // 2):
+        earlier.append(lax.ppermute(earlier[-1], axis, up))
+    for _ in range((ways - 1) // 2):
+        later.append(lax.ppermute(later[-1], axis, down))
+    line = jnp.concatenate([*earlier[::-1], *later[1:]], axis=dim)
+    return jnp.roll(line, (lax.axis_index(axis) - ways // 2) * array.shape[dim], axis=dim)
 
 
 def as_sent(shard):
@@ -83,7 +96,7 @@
     normed = (second_wide * inverse_rms[:, None] * scaling).astype(jnp.bfloat16)
     keys_whole, values_whole = (
         lax.all_gather(matchers, "ctx", axis=0, tiled=True),
-        lax.all_gather(normed, "ctx", axis=0, tiled=True),
+        collect(normed, "ctx", 0),
     )
     query_pos = position + jnp.arange(local_rows, dtype=jnp.int32)
     key_pos = jnp.arange(total_rows, dtype=jnp.int32)

time: 274 us -> 320 us (1.17)
  local copies, waits for them, and re-layouts: 35.2 us -> 51.9 us
  waiting for transfers between devices: 81 us -> 97.6 us
  starting transfers between devices: 10 us -> 18.3 us
  matrix products: 60.8 us -> 69 us
  other arithmetic: 25.2 us -> 20.6 us
    ppermute x0 -> x7, waiting for transfers between devices: none -> 27.8 us  [the longest x4 27.8 us: collect(): earlier.append(lax.ppermute(earlier[-1], axis, up))]
    unnamed x93 -> x106, local copies, waits for them, and re-layouts: 12.7 us -> 23.3 us
    ppermute x0 -> x7, starting transfers between devices: none -> 8.51 us  [the longest x3 8.12 us: collect(): later.append(lax.ppermute(later[-1], axis, down))]
    dot_general x8, matrix products: 7.84 us -> 15.4 us  [shards(): lax.dot_general(cotangent_head, value_head, contract, preferred_element_t...]
    all_gather x1 -> x0, waiting for transfers between devices: 7.58 us -> none  [shards(): lax.all_gather(normed, 'ctx', axis=0, tiled=True)]
    dot_general x8, local copies, waits for them, and re-layouts: 5.06 us -> 10.3 us  [shards(): attended = jnp.dot(weights, value_head, preferred_element_type=jnp.float32)]
    dot_general x8, matrix products: 13 us -> 9.17 us  [shards(): query_grad = jnp.dot(dscore, key_head, preferred_element_type=jnp.float32)]
    reduce_scatter x1, waiting for transfers between devices: 25.8 us -> 22.1 us  [shards(): lax.psum_scatter(jnp.concatenate([key_part.reshape(local_rows * lax.axis_...]
  transfers between devices with their start and end apart: 8 -> 14, of which waited for: 4 -> 8; matrix products, arithmetic and copies ran while one was open for 25% -> 18% of each run, Pallas kernels for 0% -> 0%
where the time goes in v1:
time: 320 us; the launch traced here: 318 us
  waiting for transfers between devices  97.6 us (30%)
  matrix products  69 us (22%)
  local copies, waits for them, and re-layouts  51.9 us (16%)
  blocking collectives  46.1 us (14%)
  other arithmetic  20.6 us (6%)
  starting transfers between devices  18.3 us (6%)
  between operations  14.7 us (5%)
    psum x1, waiting for transfers between devices, shards(): lax.psum(kernel_part.astype(jnp.bfloat16), 'ctx').astype(jnp.float32)  45.7 us
    ppermute x4, waiting for transfers between devices, collect(): earlier.append(lax.ppermute(earlier[-1], axis, up))  27.8 us
    psum x2, blocking collectives, channel_total(): return lax.psum(partial_value, 'tp')  23.8 us
    unnamed x106, local copies, waits for them, and re-layouts  23.3 us
    psum x1, blocking collectives, shards(): lax.psum(stencil_part.astype(jnp.bfloat16), 'ctx').astype(jnp.float32)  22.4 us
    reduce_scatter x1, waiting for transfers between devices, shards(): lax.psum_scatter(jnp.concatenate([key_part.reshape(local_rows * lax.axis_...  22.1 us
    conv_general_dilated x6, matrix products, depthwise(): lax.conv_general_dilated(padded[None], tap_rows[:, None, :], (1,), 'VALID...  19.9 us
    dot_general x8, matrix products, shards(): lax.dot_general(cotangent_head, value_head, contract, preferred_element_t...  15.4 us
  transfers between devices with their start and end apart: 14, of which 8 were waited for; matrix products, arithmetic and copies ran while one was open for 18% of the time, Pallas kernels for 0%

profile of v1, /device:TPU:0, one launch (start us, length us, event | category | flops | bytes accessed | tf_op | source)
XLA Modules:
  0.0 318.1 jit_solution(17302481788615317203)
XLA Ops:
  8.3 2.4 collective-permute-start
  10.7 2.8 rev.12
  16.8 4.5 %collective-permute-start.1 = (bf16[127,1024]{1,0:T(8,128)(2,1)S(1)}, bf16[127,1024]{1,0:T(8,128)(2,1)S(1)}, u32[]{:S(2)}, u32[]{:S(2)}) collective-permute-start(bf16[127,1024]{1,0:T(8,128)(2,1)S(1)} %slice.309), channel_id=1, source_target_pairs={{0,4},{4,8},{8,12},{12,16},{16,20},{20,24},{24,28},{1,5},{5,9},{9,... | collective-permute-start | bytes 780296 | tf_op jit(solution)/shard_map/ppermute | solution.py:38
  23.4 5.6 %fusion.74 = f32[1,128,1024]{2,0,1:T(1,128)S(1)} fusion(f32[1,255,1024]{2,0,1:T(1,128)S(1)} %broadcast_in_dim.33, f32[128,1,1024]{2,0,1:T(8,128)S(1)} %bitcast.165), kind=kOutput, calls=%fused_computation.133 | convolution fusion | flops 201326592 | bytes 2093056 | tf_op jit(solution)/shard_map/conv_general_dilated | solution.py:42
  29.3 12.1 %psum.35 = f32[128]{0:T(128)S(1)} all-reduce(f32[128]{0:T(128)S(1)} %get-tuple-element.63), channel_id=1, replica_groups=mesh['ctx'=8,'tp'=4] {'tp'}, use_global_device_ids=true, to_apply=%region_3.4 | all-reduce | flops 128 | bytes 1024 | tf_op jit(solution)/shard_map/psum | solution.py:58
  41.9 10.8 %collective-permute-done.2 = bf16[128,1024]{1,0:T(8,128)(2,1)S(1)} collective-permute-done((bf16[128,1024]{1,0:T(8,128)(2,1)S(1)}, bf16[128,1024]{1,0:T(8,128)(2,1)S(1)}, u32[]{:S(2)}, u32[]{:S(2)}) %collective-permute-start.2) | collective-permute-done | bytes 262176 | tf_op jit(solution)/shard_map/ppermute | solution.py:20
  52.7 2.6 collective-permute-start.6
  55.4 6.8 %collective-permute-done.3 = bf16[128,1024]{1,0:T(8,128)(2,1)S(1)} collective-permute-done((bf16[128,1024]{1,0:T(8,128)(2,1)S(1)}, bf16[128,1024]{1,0:T(8,128)(2,1)S(1)}, u32[]{:S(2)}, u32[]{:S(2)}) %collective-permute-start.3) | collective-permute-done | bytes 262176 | tf_op jit(solution)/shard_map/ppermute | solution.py:20
  62.2 2.6 collective-permute-start.7
  64.8 6.0 %collective-permute-done.4 = bf16[128,1024]{1,0:T(8,128)(2,1)S(1)} collective-permute-done((bf16[128,1024]{1,0:T(8,128)(2,1)S(1)}, bf16[128,1024]{1,0:T(8,128)(2,1)S(1)}, u32[]{:S(2)}, u32[]{:S(2)}) %collective-permute-start.4) | collective-permute-done | bytes 262176 | tf_op jit(solution)/shard_map/ppermute | solution.py:20
  72.9 2.8 collective-permute-start.8
  75.7 4.2 %collective-permute-done.5 = bf16[128,1024]{1,0:T(8,128)(2,1)S(1)} collective-permute-done((bf16[128,1024]{1,0:T(8,128)(2,1)S(1)}, bf16[128,1024]{1,0:T(8,128)(2,1)S(1)}, u32[]{:S(2)}, u32[]{:S(2)}) %collective-permute-start.5) | collective-permute-done | bytes 262176 | tf_op jit(solution)/shard_map/ppermute | solution.py:20
  132.8 2.6 copy.114
  135.4 2.3 convolution_convert_fusion
  137.7 2.6 copy.116
  140.3 4.7 %pad_maximum_fusion = bf16[1024,2048]{1,0:T(8,128)(2,1)} fusion(bf16[1024,1024]{1,0:T(8,128)(2,1)} %copy.116, bf16[1024,1024]{1,0:T(8,128)(2,1)} %copy.114), kind=kLoop, calls=%fused_computation | loop fusion | flops 8388608 | bytes 8388608 | tf_op jit(solution)/shard_map/concatenate | solution.py:156
  173.7 22.1 %reduce-scatter.2.cloned.1.call-done = bf16[128,2048]{1,0:T(8,128)(2,1)} async-done(((bf16[1024,2048]{1,0:T(8,128)(2,1)}), bf16[128,2048]{1,0:T(8,128)(2,1)}) %reduce-scatter.2.cloned.1.call-update) | async-done | bytes 524304 | tf_op jit(solution)/shard_map/reduce_scatter | solution.py:155
  196.9 11.7 %psum.36 = f32[128]{0:T(128)S(1)} all-reduce(f32[128]{0:T(128)S(1)} %get-tuple-element.34), channel_id=1, replica_groups=mesh['ctx'=8,'tp'=4] {'tp'}, use_global_device_ids=true, to_apply=%region_28.29 | all-reduce | flops 128 | bytes 1024 | tf_op jit(solution)/shard_map/psum | solution.py:58
  209.8 6.8 %fusion.70 = bf16[1,128,1024]{2,0,1:T(2,128)(2,1)S(1)} fusion(f32[1,255,1024]{2,0,1:T(1,128)} %copy-done.26, f32[128,1,1024]{2,0,1:T(8,128)S(1)} %bitcast.159), kind=kOutput, calls=%fused_computation.129 | convolution fusion | flops 201326592 | bytes 1830912 | tf_op jit(solution)/shard_map/conv_general_dilated | solution.py:42
  216.8 2.6 rev.15
  224.6 45.7 %all-reduce.3.cloned.1.call-done = bf16[128,1024]{1,0:T(8,128)(2,1)} async-done(((bf16[128,1024]{1,0:T(8,128)(2,1)}), bf16[128,1024]{1,0:T(8,128)(2,1)}) %all-reduce.3.cloned.1.call-update) | async-done | bytes 262160 | tf_op jit(solution)/shard_map/psum | solution.py:193
  272.3 5.8 %fusion.40 = f32[1,128,1024]{2,0,1:T(1,128)S(1)} fusion(f32[1,255,1024]{2,1,0:T(8,128)S(1)} %maximum_bitcast_fusion, f32[128,1,1024]{2,0,1:T(8,128)S(1)} %bitcast.164), kind=kOutput, calls=%fused_computation.77 | convolution fusion | flops 201326592 | bytes 2093056 | tf_op jit(solution)/shard_map/conv_general_dilated | solution.py:42
  278.1 2.7 multiply_convert_fusion
  282.4 22.4 %all-reduce = (bf16[7,1024]{1,0:T(8,128)(2,1)S(1)}, bf16[1024]{0:T(1024)(128)(2,1)S(1)}) all-reduce(bf16[7,1024]{1,0:T(8,128)(2,1)S(1)} %rev.14, bf16[1024]{0:T(1024)(128)(2,1)S(1)} %get-tuple-element.33), channel_id=1, replica_groups=mesh['ctx'=8,'tp'=4] {'ctx'}, use_global_device_ids=true, to_apply=%region_29.30 | all-reduce | flops 8192 | bytes 32768 | tf_op jit(solution)/shard_map/psum | solution.py:192
  (242 shorter events, 108.3 us)
Async XLA Ops:
  7.2 84.6 %all-gather.2.cloned.1.call-start = ((), (), s32[]{:S(2)}) async-start(), calls=%async_computation.1 | async-start | bytes 2359296 | tf_op jit(solution)/shard_map/all_gather | solution.py:98
  8.3 5.2 %collective-permute-start = (bf16[6,1024]{1,0:T(8,128)(2,1)S(1)}, bf16[6,1024]{1,0:T(8,128)(2,1)S(1)}, u32[]{:S(2)}, u32[]{:S(2)}) collective-permute-start(bf16[6,1024]{1,0:T(8,128)(2,1)S(1)} %slice.311), channel_id=1, source_target_pairs={{0,4},{4,8},{8,12},{12,16},{16,20},{20,24},{24,28},{1,5},{5,9},{9,... | collective-permute-start | bytes 36872 | tf_op jit(solution)/shard_map/ppermute | solution.py:38
  16.8 5.7 %collective-permute-start.1 = (bf16[127,1024]{1,0:T(8,128)(2,1)S(1)}, bf16[127,1024]{1,0:T(8,128)(2,1)S(1)}, u32[]{:S(2)}, u32[]{:S(2)}) collective-permute-start(bf16[127,1024]{1,0:T(8,128)(2,1)S(1)} %slice.309), channel_id=1, source_target_pairs={{0,4},{4,8},{8,12},{12,16},{16,20},{20,24},{24,28},{1,5},{5,9},{9,... | collective-permute-start | bytes 780296 | tf_op jit(solution)/shard_map/ppermute | solution.py:38
  21.4 174.3 %reduce-scatter.2.cloned.1.call-start = ((), (), s32[]{:S(2)}) async-start(), calls=%async_computation.2 | async-start | bytes 4718592 | tf_op jit(solution)/shard_map/reduce_scatter | solution.py:155
  23.4 18.0 %copy-start.37 = (f32[1024]{0:T(1024)S(1)}, f32[1024]{0:T(1024)}, u32[]{:S(2)}) copy-start(f32[1024]{0:T(1024)} %param.19) | copy-start | bytes 12292
  29.0 53.0 %copy-start.8 = (f32[1,128,1024]{2,0,1:T(1,128)}, f32[1,128,1024]{2,0,1:T(1,128)S(1)}, u32[]{:S(2)}) copy-start(f32[1,128,1024]{2,0,1:T(1,128)S(1)} %fusion.74) | copy-start | bytes 1572868
  29.1 41.8 %copy-start.1 = (bf16[128,1024]{1,0:T(8,128)(2,1)S(1)}, bf16[128,1024]{1,0:T(8,128)(2,1)}, u32[]{:S(2)}) copy-start(bf16[128,1024]{1,0:T(8,128)(2,1)} %param.23) | copy-start | bytes 786436
  29.1 43.8 %copy-start.39 = (s32[1024]{0:T(1024)S(1)}, s32[1024]{0:T(1024)}, u32[]{:S(2)}) copy-start(s32[1024]{0:T(1024)} %param.22) | copy-start | bytes 12292
  41.6 11.2 %collective-permute-start.2 = (bf16[128,1024]{1,0:T(8,128)(2,1)S(1)}, bf16[128,1024]{1,0:T(8,128)(2,1)S(1)}, u32[]{:S(2)}, u32[]{:S(2)}) collective-permute-start(bf16[128,1024]{1,0:T(8,128)(2,1)S(1)} %fusion.64), channel_id=1, source_target_pairs={{0,4},{4,8},{8,12},{12,16},{16,20},{20,24},{24,28},{28,0},{1,5},{5... | collective-permute-start | bytes 786440 | tf_op jit(solution)/shard_map/ppermute | solution.py:20
  52.7 9.5 %collective-permute-start.3 = (bf16[128,1024]{1,0:T(8,128)(2,1)S(1)}, bf16[128,1024]{1,0:T(8,128)(2,1)S(1)}, u32[]{:S(2)}, u32[]{:S(2)}) collective-permute-start(bf16[128,1024]{1,0:T(8,128)(2,1)S(1)} %collective-permute-done.2), channel_id=1, source_target_pairs={{0,4},{4,8},{8,12},{12,16},{16,20},{20,24},{24,28},{28,0},{1,5},{5... | collective-permute-start | bytes 786440 | tf_op jit(solution)/shard_map/ppermute | solution.py:20
  52.7 9.5 %collective-permute-start.6 = (bf16[128,1024]{1,0:T(8,128)(2,1)S(1)}, bf16[128,1024]{1,0:T(8,128)(2,1)S(1)}, u32[]{:S(2)}, u32[]{:S(2)}) collective-permute-start(bf16[128,1024]{1,0:T(8,128)(2,1)S(1)} %fusion.64), channel_id=1, source_target_pairs={{0,28},{4,0},{8,4},{12,8},{16,12},{20,16},{24,20},{28,24},{1,29},{... | collective-permute-start | bytes 786440 | tf_op jit(solution)/shard_map/ppermute | solution.py:22
  62.2 8.7 %collective-permute-start.4 = (bf16[128,1024]{1,0:T(8,128)(2,1)S(1)}, bf16[128,1024]{1,0:T(8,128)(2,1)S(1)}, u32[]{:S(2)}, u32[]{:S(2)}) collective-permute-start(bf16[128,1024]{1,0:T(8,128)(2,1)S(1)} %collective-permute-done.3), channel_id=1, source_target_pairs={{0,4},{4,8},{8,12},{12,16},{16,20},{20,24},{24,28},{28,0},{1,5},{5... | collective-permute-start | bytes 786440 | tf_op jit(solution)/shard_map/ppermute | solution.py:20
  62.2 10.7 %collective-permute-start.7 = (bf16[128,1024]{1,0:T(8,128)(2,1)S(1)}, bf16[128,1024]{1,0:T(8,128)(2,1)S(1)}, u32[]{:S(2)}, u32[]{:S(2)}) collective-permute-start(bf16[128,1024]{1,0:T(8,128)(2,1)S(1)} %collective-permute-done.6), channel_id=1, source_target_pairs={{0,28},{4,0},{8,4},{12,8},{16,12},{20,16},{24,20},{28,24},{1,29},{... | collective-permute-start | bytes 786440 | tf_op jit(solution)/shard_map/ppermute | solution.py:22
  70.8 9.1 %collective-permute-start.5 = (bf16[128,1024]{1,0:T(8,128)(2,1)S(1)}, bf16[128,1024]{1,0:T(8,128)(2,1)S(1)}, u32[]{:S(2)}, u32[]{:S(2)}) collective-permute-start(bf16[128,1024]{1,0:T(8,128)(2,1)S(1)} %collective-permute-done.4), channel_id=1, source_target_pairs={{0,4},{4,8},{8,12},{12,16},{16,20},{20,24},{24,28},{28,0},{1,5},{5... | collective-permute-start | bytes 786440 | tf_op jit(solution)/shard_map/ppermute | solution.py:20
  72.9 12.2 %collective-permute-start.8 = (bf16[128,1024]{1,0:T(8,128)(2,1)S(1)}, bf16[128,1024]{1,0:T(8,128)(2,1)S(1)}, u32[]{:S(2)}, u32[]{:S(2)}) collective-permute-start(bf16[128,1024]{1,0:T(8,128)(2,1)S(1)} %collective-permute-done.7), channel_id=1, source_target_pairs={{0,28},{4,0},{8,4},{12,8},{16,12},{20,16},{24,20},{28,24},{1,29},{... | collective-permute-start | bytes 786440 | tf_op jit(solution)/shard_map/ppermute | solution.py:22
  144.9 19.5 %copy-start.10 = (bf16[1024,1024]{1,0:T(8,128)(2,1)S(1)}, bf16[1024,1024]{1,0:T(8,128)(2,1)}, u32[]{:S(2)}) copy-start(bf16[1024,1024]{1,0:T(8,128)(2,1)} %all-gather.2.cloned.1.call-done) | copy-start | bytes 6291460
  144.9 19.5 %copy-start.13 = (bf16[128,1024]{1,0:T(8,128)(2,1)S(1)}, bf16[128,1024]{1,0:T(8,128)(2,1)}, u32[]{:S(2)}) copy-start(bf16[128,1024]{1,0:T(8,128)(2,1)} %get-tuple-element.90) | copy-start | bytes 786436
  145.0 125.4 %all-reduce.3.cloned.1.call-start = ((), (), s32[]{:S(2)}) async-start(), calls=%async_computation.3 | async-start | bytes 524288 | tf_op jit(solution)/shard_map/psum | solution.py:193
  155.5 15.5 %copy-start.16 = (bf16[128,1024]{1,0:T(8,128)(2,1)S(1)}, bf16[128,1024]{1,0:T(8,128)(2,1)}, u32[]{:S(2)}) copy-start(bf16[128,1024]{1,0:T(8,128)(2,1)} %get-tuple-element.100) | copy-start | bytes 786436
  155.5 16.4 %copy-start.17 = (bf16[128,1024]{1,0:T(8,128)(2,1)S(1)}, bf16[128,1024]{1,0:T(8,128)(2,1)}, u32[]{:S(2)}) copy-start(bf16[128,1024]{1,0:T(8,128)(2,1)} %get-tuple-element.102) | copy-start | bytes 786436
  165.4 43.2 %copy-start.20 = (bf16[128,1024]{1,0:T(8,128)(2,1)S(1)}, bf16[128,1024]{1,0:T(8,128)(2,1)}, u32[]{:S(2)}) copy-start(bf16[128,1024]{1,0:T(8,128)(2,1)} %param.16) | copy-start | bytes 786436
  220.2 51.9 %collective-permute-start.9 = (bf16[127,1024]{1,0:T(8,128)(2,1)S(1)}, bf16[127,1024]{1,0:T(8,128)(2,1)S(1)}, u32[]{:S(2)}, u32[]{:S(2)}) collective-permute-start(bf16[127,1024]{1,0:T(8,128)(2,1)S(1)} %slice.308), channel_id=1, source_target_pairs={{4,0},{8,4},{12,8},{16,12},{20,16},{24,20},{28,24},{5,1},{9,5},{13... | collective-permute-start | bytes 780296 | tf_op jit(solution)/shard_map/ppermute | solution.py:38
  223.9 48.4 %copy-start.34 = (f32[128,1024]{1,0:T(8,128)S(1)}, f32[128,1024]{1,0:T(8,128)}, u32[]{:S(2)}) copy-start(f32[128,1024]{1,0:T(8,128)} %param.18) | copy-start | bytes 1572868
  305.4 3.1 collective-permute-start.10
  (31 other events, 185.9 us)
Sparse Core Ops, SparseCore 0:
  21.5 30.9 all-gather.1
  145.1 50.6 reduce-scatter.1
  219.5 50.7 all-reduce.2
